TPU v7x, 128 devices: a whole 4x4x4 slice. The times are simulated.
128 devices in a mesh: expert: 32 (over y, z, core), dp: 4 (over x).
Axes of the slice: x: 4, y: 4, z: 4, core: 2. Of those that a mesh axis runs over, the one named last changes fastest.
Arguments:
- activations: bfloat16 [2048, 7168], P(('expert', 'dp')), may hold values from -6 to 6
- cotangent: bfloat16 [2048, 7168], P(('expert', 'dp')), may hold values from -6 to 6
- route_ids: int32 [2048, 8], P(('expert', 'dp')), may hold values from 0 to 31, all different within a row; in each aligned block of 16 rows (0 to 15, 16 to 31, ...) at most 5 rows name the same one
- route_weights: float32 [2048, 8], P(('expert', 'dp')), may hold values from 0.05 to 0.6
- gate_weights: bfloat16 [32, 7168, 1024], P('expert', 'dp'), may hold values from -0.0625 to 0.0625
- up_weights: bfloat16 [32, 7168, 1024], P('expert', 'dp'), may hold values from -0.0625 to 0.0625
- down_weights: bfloat16 [32, 1024, 7168], P('expert', None, 'dp'), may hold values from -0.1875 to 0.1875
Outputs:
- grad_input: bfloat16 [2048, 7168], P(('expert', 'dp'))
- grad_gate: bfloat16 [32, 7168, 1024], P('expert', 'dp')
- grad_up: bfloat16 [32, 7168, 1024], P('expert', 'dp')
- grad_down: bfloat16 [32, 1024, 7168], P('expert', None, 'dp')
Inputs may be any that keep to these rules, and one draw needn't show every extreme that they name: `route_ids`: each token names 8 different experts. Among the routes of one device's 16 tokens, no expert is named more than 5 times, a bound that some block reaches.
All inputs are finite; a program needn't handle non-finite values.
Results may differ from a plain program's by a relative error of at most 0.0064.
Values may be sent and summed in bfloat16 or wider, within the bound.
No kernel may reach another device: no remote copies, remote signals or barrier semaphores. Data moves between devices by JAX's collectives and lax.ppermute only.
A program may use at most 128 MiB of HBM per device.

v0:
```python
import jax
import jax.numpy as jnp
from jax import lax
from jax.sharding import PartitionSpec as P


def swiglu_back(gate, upper, upstream):
    sigma = jax.nn.sigmoid(gate)
    silu_gate = gate * sigma
    activated = (silu_gate * upper).astype(jnp.bfloat16)
    grad_pre = (upstream * upper * sigma * (1.0 + gate * (1.0 - sigma))).astype(jnp.bfloat16)
    grad_lin = (upstream * silu_gate).astype(jnp.bfloat16)
    return (grad_pre, grad_lin, activated)


def contract_rows(left, right):
    return lax.dot_general(
        left, right, (((0,), (0,)), ((), ())), preferred_element_type=jnp.float32
    )


def shards(
    activations, cotangent, route_ids, route_weights, gate_weights, up_weights, down_weights
):
    tok_rows, width = activations.shape
    topk = route_ids.shape[1]
    num_dp = lax.axis_size("dp")
    num_exp = lax.axis_size("expert")
    slice_width = gate_weights.shape[1]
    hidden = gate_weights.shape[2]
    capacity = min(tok_rows, 5 * tok_rows * topk // (4 * num_exp))
    buffer_rows = num_exp * num_dp * capacity
    flat_ids = route_ids.reshape(-1)
    expert_iota = jnp.arange(num_exp, dtype=jnp.int32)
    onehot = (flat_ids[:, None] == expert_iota[None, :]).astype(jnp.int32)
    before = jnp.cumsum(onehot, axis=0) - onehot
    slot = jnp.sum(before * onehot, axis=1)
    target = (flat_ids * capacity + slot).reshape(tok_rows, topk)
    slot_iota = jnp.arange(num_exp * capacity, dtype=jnp.int32)
    matches = target[:, :, None] == slot_iota[None, None, :]
    placing = jnp.any(matches, axis=1).astype(jnp.bfloat16)
    slot_weight = jnp.sum(jnp.where(matches, route_weights[:, :, None], 0.0), axis=(0, 1))
    send_act = contract_rows(placing, activations).astype(jnp.bfloat16)
    send_cot = (contract_rows(placing, cotangent) * slot_weight[:, None]).astype(jnp.bfloat16)
    send_act = send_act.reshape(num_exp, capacity, num_dp, slice_width)
    send_cot = send_cot.reshape(num_exp, capacity, num_dp, slice_width)
    send_both = jnp.concatenate([send_act, send_cot], axis=3)
    flat_both = jnp.swapaxes(send_both, 1, 2).reshape(num_exp * num_dp, capacity, 2 * slice_width)
    recv_both = lax.all_to_all(flat_both, ("expert", "dp"), split_axis=0, concat_axis=0, tiled=True)
    recv_both = recv_both.reshape(buffer_rows, 2 * slice_width)
    act_rows = recv_both[:, :slice_width]
    cot_rows = recv_both[:, slice_width:]
    gate_local = gate_weights[0]
    up_local = up_weights[0]
    down_local = down_weights[0]
    gate_part = jnp.dot(act_rows, gate_local, preferred_element_type=jnp.float32)
    up_part = jnp.dot(act_rows, up_local, preferred_element_type=jnp.float32)
    back_part = lax.dot_general(
        cot_rows, down_local, (((1,), (1,)), ((), ())), preferred_element_type=jnp.float32
    )
    summed = lax.psum_scatter(
        jnp.concatenate([gate_part, up_part, back_part], axis=1),
        "dp",
        scatter_dimension=0,
        tiled=True,
    )
    grad_pre, grad_lin, activated = swiglu_back(
        summed[:, :hidden], summed[:, hidden : 2 * hidden], summed[:, 2 * hidden :]
    )
    gathered = lax.all_gather(
        jnp.concatenate([grad_pre, grad_lin, activated], axis=1), "dp", axis=0, tiled=True
    )
    grad_pre = gathered[:, :hidden]
    grad_lin = gathered[:, hidden : 2 * hidden]
    activated = gathered[:, 2 * hidden :]
    rows_back = lax.dot_general(
        grad_pre, gate_local, (((1,), (1,)), ((), ())), preferred_element_type=jnp.float32
    ) + lax.dot_general(
        grad_lin, up_local, (((1,), (1,)), ((), ())), preferred_element_type=jnp.float32
    )
    grad_gate = contract_rows(act_rows, grad_pre).astype(jnp.bfloat16)[None]
    grad_up = contract_rows(act_rows, grad_lin).astype(jnp.bfloat16)[None]
    grad_down = contract_rows(activated, cot_rows).astype(jnp.bfloat16)[None]
    back_rows = rows_back.astype(jnp.bfloat16)
    flat_back = back_rows.reshape(num_exp * num_dp, capacity, slice_width)
    arrived = lax.all_to_all(flat_back, ("expert", "dp"), split_axis=0, concat_axis=0, tiled=True)
    arrived = jnp.swapaxes(arrived.reshape(num_exp, num_dp, capacity, slice_width), 1, 2)
    arrived = arrived.reshape(num_exp * capacity, width)
    grad_input = jnp.dot(placing, arrived, preferred_element_type=jnp.float32).astype(jnp.bfloat16)
    return (grad_input, grad_gate, grad_up, grad_down)


def solution(mesh):
    placed = (
        P(("expert", "dp"), None),
        P(("expert", "dp"), None),
        P(("expert", "dp"), None),
        P(("expert", "dp"), None),
        P("expert", "dp", None),
        P("expert", "dp", None),
        P("expert", None, "dp"),
    )
    return jax.shard_map(
        shards,
        mesh=mesh,
        in_specs=placed,
        out_specs=(
            P(("expert", "dp"), None),
            P("expert", "dp", None),
            P("expert", "dp", None),
            P("expert", None, "dp"),
        ),
        check_vma=False,
    )
```

profile of v0, /device:TPU:1, one launch (start us, length us, event | category | flops | bytes accessed | tf_op | source)
XLA Modules:
  0.0 347.9 jit_solution(13178940153341892583)
XLA Ops:
  7.2 0.0 copy-start
  7.2 0.0 reduce-scatter.2.cloned.1.call-start
  7.2 0.8 copy.28
  8.0 0.1 eq.28
  8.1 0.1 fusion.29
  8.2 0.0 copy-start.3
  8.2 0.2 reduce_window_sum.11
  8.4 0.2 select_reduce_fusion.1
  8.6 0.1 reduce_sum.21
  8.7 0.1 fusion.28
  8.8 0.8 copy.30
  9.6 0.1 select_reduce_fusion
  9.7 0.0 copy-done
  9.7 2.2 fusion
  11.9 3.5 reshape.40
  15.4 0.0 copy-done.3
  15.4 2.2 convolution_convert_fusion
  17.6 4.6 %reshape.39 = bf16[32,5,4,1792]{3,2,1,0:T(4,128)(2,1)} reshape(bf16[160,7168]{1,0:T(8,128)(2,1)} %convolution_convert_fusion) | data formatting | bytes 4587520 | tf_op jit(solution)/shard_map/reshape | solution.py:45
  22.2 3.7 %maximum_bitcast_fusion = bf16[32,4,5,3584]{3,1,2,0:T(4,128)(2,1)S(1)} fusion(bf16[32,5,4,1792]{3,2,1,0:T(4,128)(2,1)S(1)} %reshape.40, bf16[32,5,4,1792]{3,2,1,0:T(4,128)(2,1)} %reshape.39), kind=kLoop, calls=%fused_computation.5 | loop fusion | flops 9175040 | bytes 9175040 | tf_op jit(solution)/shard_map/transpose | solution.py:48
  25.9 1.7 copy.36
  27.6 98.5 %all_to_all.10 = bf16[128,5,3584]{2,1,0:T(8,128)(2,1)} all-to-all(bf16[128,5,3584]{2,1,0:T(8,128)(2,1)S(1)} %bitcast.36), channel_id=1, replica_groups=mesh['expert'=32,'dp'=4] {'expert','dp'}, dimensions={0} | all-to-all | bytes 9175040 | tf_op jit(solution)/shard_map/all_to_all | solution.py:49
  126.1 8.1 %reshape.42 = bf16[640,3584]{1,0:T(8,128)(2,1)} reshape(bf16[128,5,3584]{2,1,0:T(8,128)(2,1)} %all_to_all.10) | data formatting | bytes 9175040 | tf_op jit(solution)/shard_map/reshape | solution.py:50
  134.2 0.0 copy-start.2
  134.2 0.0 copy-start.6
  134.2 5.4 %fusion.1 = f32[640,1024]{1,0:T(8,128)S(1)} fusion(bf16[1,1024,1792]{2,1,0:T(8,128)(2,1)} %param.13, bf16[640,3584]{1,0:T(8,128)(2,1)} %reshape.42), kind=kOutput, calls=%fused_computation.10 | convolution fusion | flops 2348810240 | bytes 8585216 | tf_op jit(solution)/shard_map/dot_general | solution.py:58
  139.7 0.0 copy-done.2
  139.7 0.0 copy-done.6
  139.7 0.0 copy-start.7
  139.7 2.5 fusion.5
  142.2 0.0 copy-done.7
  142.2 2.5 fusion.9
  144.8 3.4 pad_maximum_fusion
  148.2 0.0 reduce-scatter.2.cloned.1.call-update
  148.2 0.0 all-gather.2.cloned.1.call-start
  148.3 72.4 %reduce-scatter.2.cloned.1.call-done = f32[160,3072]{1,0:T(8,128)} async-done(((f32[640,3072]{1,0:T(8,128)}), f32[160,3072]{1,0:T(8,128)}) %reduce-scatter.2.cloned.1.call-update) | async-done | bytes 1966096 | tf_op jit(solution)/shard_map/reduce_scatter | solution.py:61
  220.7 1.9 multiply_convert_fusion.2
  222.6 1.0 pad_maximum_fusion.1
  223.6 0.0 all-gather.2.cloned.1.call-update
  223.7 45.8 %all-gather.2.cloned.1.call-done = bf16[640,3072]{1,0:T(8,128)(2,1)} async-done(((bf16[160,3072]{1,0:T(8,128)(2,1)}), bf16[640,3072]{1,0:T(8,128)(2,1)}) %all-gather.2.cloned.1.call-update) | async-done | bytes 3932176 | tf_op jit(solution)/shard_map/all_gather | solution.py:70
  269.4 0.0 copy-start.4
  269.4 0.0 copy-start.8
  269.4 5.2 %fusion.3 = f32[640,1792]{1,0:T(8,128)S(1)} fusion(bf16[1,1792,1024]{2,1,0:T(8,128)(2,1)} %param.12, bf16[640,3072]{1,0:T(8,128)(2,1)} %all-gather.2.cloned.1.call-done), kind=kOutput, calls=%fused_computation.12 | convolution fusion | flops 2348810240 | bytes 9568256 | tf_op jit(solution)/shard_map/dot_general | solution.py:78
  274.6 0.0 copy-done.4
  274.6 0.0 copy-done.8
  274.6 2.6 add_convert_fusion
  277.2 2.7 reshape.43
  279.9 0.0 slice-start
  279.9 9.2 %all-to-all-start.1 = ((bf16[128,5,1792]{2,1,0:T(8,128)(2,1)}), bf16[128,5,1792]{2,1,0:T(8,128)(2,1)}, u32[]{:S(2)}, u32[]{:S(2)}) async-start(bf16[128,5,1792]{2,1,0:T(8,128)(2,1)} %reshape.43), calls=%async_computation.2 | async-start | bytes 7340032 | tf_op jit(solution)/shard_map/all_to_all | solution.py:86
  289.1 0.0 slice-start.1
  289.1 0.0 copy-start.5
  289.1 7.1 %fusion.11 = bf16[1,1792,1024]{2,1,0:T(8,128)(2,1)} fusion(bf16[640,3584]{1,0:T(8,128)(2,1)} %reshape.42, bf16[640,3072]{1,0:T(8,128)(2,1)} %all-gather.2.cloned.1.call-done), kind=kOutput, calls=%fused_computation.20 | convolution fusion | flops 2350645248 | bytes 7274496 | tf_op jit(solution)/shard_map/dot_general | solution.py:17
  296.2 0.0 slice-done
  296.2 0.0 slice-done.1
  296.2 0.0 copy-done.5
  296.2 4.5 %fusion.12 = bf16[1,1792,1024]{2,1,0:T(8,128)(2,1)} fusion(bf16[640,3584]{1,0:T(8,128)(2,1)S(1)} %bitcast.40, bf16[640,3072]{1,0:T(8,128)(2,1)S(1)} %copy-done.5), kind=kOutput, calls=%fused_computation.21 | convolution fusion | flops 2350645248 | bytes 7274496 | tf_op jit(solution)/shard_map/dot_general | solution.py:17
  300.8 4.5 %fusion.13 = bf16[1,1024,1792]{2,1,0:T(8,128)(2,1)} fusion(bf16[640,3584]{1,0:T(8,128)(2,1)S(1)} %bitcast.40, bf16[640,3072]{1,0:T(8,128)(2,1)S(1)} %copy-done.5), kind=kOutput, calls=%fused_computation.22 | convolution fusion | flops 2350645248 | bytes 7274496 | tf_op jit(solution)/shard_map/dot_general | solution.py:17
  305.3 31.4 %all-to-all-done.1 = bf16[128,5,1792]{2,1,0:T(8,128)(2,1)} async-done(((bf16[128,5,1792]{2,1,0:T(8,128)(2,1)}), bf16[128,5,1792]{2,1,0:T(8,128)(2,1)}, u32[]{:S(2)}, u32[]{:S(2)}) %all-to-all-start.1) | async-done | bytes 2293792 | tf_op jit(solution)/shard_map/all_to_all | solution.py:86
  336.6 0.0 copy-start.1
  336.6 3.0 copy.34
  339.7 0.3 copy.38
  340.0 1.1 convolution_convert_fusion.1
  341.1 0.0 copy-done.1
  (2 shorter events, 0.0 us)
Async XLA Ops:
  7.2 2.5 copy-start
  7.2 213.5 %reduce-scatter.2.cloned.1.call-start = ((), (), s32[]{:S(2)}) async-start(), calls=%async_computation.3 | async-start | bytes 9830400 | tf_op jit(solution)/shard_map/reduce_scatter | solution.py:61
  8.2 7.2 %copy-start.3 = (bf16[16,7168]{1,0:T(8,128)(2,1)S(1)}, bf16[16,7168]{1,0:T(8,128)(2,1)}, u32[]{:S(2)}) copy-start(bf16[16,7168]{1,0:T(8,128)(2,1)} %param.7) | copy-start | bytes 688132
  134.2 5.4 %copy-start.2 = (bf16[640,3584]{1,0:T(8,128)(2,1)S(1)}, bf16[640,3584]{1,0:T(8,128)(2,1)}, u32[]{:S(2)}) copy-start(bf16[640,3584]{1,0:T(8,128)(2,1)} %reshape.42) | copy-start | bytes 13762564
  134.2 5.5 %copy-start.6 = (bf16[1,1792,1024]{2,1,0:T(8,128)(2,1)S(1)}, bf16[1,1792,1024]{2,1,0:T(8,128)(2,1)}, u32[]{:S(2)}) copy-start(bf16[1,1792,1024]{2,1,0:T(8,128)(2,1)} %param.12) | copy-start | bytes 11010052
  139.7 2.5 copy-start.7
  148.2 121.2 %all-gather.2.cloned.1.call-start = ((), (), s32[]{:S(2)}) async-start(), calls=%async_computation.4 | async-start | bytes 4915200 | tf_op jit(solution)/shard_map/all_gather | solution.py:70
  269.4 5.2 %copy-start.4 = (bf16[640,3072]{1,0:T(8,128)(2,1)S(1)}, bf16[640,3072]{1,0:T(8,128)(2,1)}, u32[]{:S(2)}) copy-start(bf16[640,3072]{1,0:T(8,128)(2,1)} %all-gather.2.cloned.1.call-done) | copy-start | bytes 11796484
  269.4 5.2 %copy-start.8 = (bf16[1,1792,1024]{2,1,0:T(8,128)(2,1)S(1)}, bf16[1,1792,1024]{2,1,0:T(8,128)(2,1)}, u32[]{:S(2)}) copy-start(bf16[1,1792,1024]{2,1,0:T(8,128)(2,1)} %param.11) | copy-start | bytes 11010052
  279.9 16.3 %slice-start = ((s8[4587520]{0:T(1024)(128)(4,1)}), s8[393216]{0:T(1024)(128)(4,1)S(1)}, s32[]{:S(2)}) async-start(s8[4587520]{0:T(1024)(128)(4,1)} %bitcast.39), calls=%async_computation.5 | async-start | bytes 786432
  279.9 56.7 %all-to-all-start.1 = ((bf16[128,5,1792]{2,1,0:T(8,128)(2,1)}), bf16[128,5,1792]{2,1,0:T(8,128)(2,1)}, u32[]{:S(2)}, u32[]{:S(2)}) async-start(bf16[128,5,1792]{2,1,0:T(8,128)(2,1)} %reshape.43), calls=%async_computation.2 | async-start | bytes 7340032 | tf_op jit(solution)/shard_map/all_to_all | solution.py:86
  289.1 7.1 %slice-start.1 = ((s8[4587520]{0:T(1024)(128)(4,1)}), s8[4194304]{0:T(1024)(128)(4,1)S(1)}, s32[]{:S(2)}) async-start(s8[4587520]{0:T(1024)(128)(4,1)} %bitcast.39), calls=%async_computation.6 | async-start | bytes 8388608
  289.1 7.1 %copy-start.5 = (bf16[640,3072]{1,0:T(8,128)(2,1)S(1)}, bf16[640,3072]{1,0:T(8,128)(2,1)}, u32[]{:S(2)}) copy-start(bf16[640,3072]{1,0:T(8,128)(2,1)} %all-gather.2.cloned.1.call-done) | copy-start | bytes 11796484
  336.6 4.5 %copy-start.1 = (bf16[16,7168]{1,0:T(8,128)(2,1)S(1)}, bf16[16,7168]{1,0:T(8,128)(2,1)}, u32[]{:S(2)}) copy-start(bf16[16,7168]{1,0:T(8,128)(2,1)} %param.8) | copy-start | bytes 688132
Sparse Core Ops, SparseCore 0:
  148.3 72.2 reduce-scatter.1
  223.8 45.6 all-gather.1
where the time goes:
time: 349 us; the launch traced here: 348 us
  waiting for transfers between devices  150 us (43%)
  blocking collectives  98.5 us (28%)
  matrix products  39.8 us (11%)
  local copies, waits for them, and re-layouts  25.7 us (7%)
  between operations  14.3 us (4%)
  other arithmetic  10.8 us (3%)
  starting transfers between devices  9.26 us (3%)
    all_to_all x1, blocking collectives, shards(): lax.all_to_all(flat_both, ('expert', 'dp'), split_axis=0, concat_axis=0,...  98.5 us
    reduce_scatter x1, waiting for transfers between devices, shards(): lax.psum_scatter(jnp.concatenate([gate_part, up_part, back_part], axis=1)...  72.4 us
    all_gather x1, waiting for transfers between devices, shards(): lax.all_gather(jnp.concatenate([grad_pre, grad_lin, activated], axis=1),...  45.8 us
    all_to_all x1, waiting for transfers between devices, shards(): lax.all_to_all(flat_back, ('expert', 'dp'), split_axis=0, concat_axis=0,...  31.4 us
    dot_general x5, matrix products, contract_rows(): lax.dot_general(left, right, (((0,), (0,)), ((), ())), preferred_element_...  20.5 us
    all_to_all x1, starting transfers between devices, shards(): lax.all_to_all(flat_back, ('expert', 'dp'), split_axis=0, concat_axis=0,...  9.18 us
    reshape x1, local copies, waits for them, and re-layouts, shards(): recv_both = recv_both.reshape(buffer_rows, 2 * slice_width)  8.11 us
  transfers between devices with their start and end apart: 3, of which 3 were waited for; matrix products, arithmetic and copies ran while one was open for 5% of the time, Pallas kernels for 0%

commit v1 on v0

--- a/solution.py
+++ b/solution.py
@@ -67,9 +67,23 @@
     grad_pre, grad_lin, activated = swiglu_back(
         summed[:, :hidden], summed[:, hidden : 2 * hidden], summed[:, 2 * hidden :]
     )
-    gathered = lax.all_gather(
-        jnp.concatenate([grad_pre, grad_lin, activated], axis=1), "dp", axis=0, tiled=True
+    shard = jnp.concatenate([grad_pre, grad_lin, activated], axis=1)
+    ways, here, step = (lax.axis_size("dp"), lax.axis_index("dp"), shard.shape[0])
+    dims = [n * ways if d == 0 else n for d, n in enumerate(shard.shape)]
+    gathered = lax.dynamic_update_slice_in_dim(
+        jnp.zeros(dims, shard.dtype), shard, here * step, axis=0
     )
+    going_up = going_down = shard
+    for far in range(1, ways // 2 + 1):
+        going_up = lax.ppermute(going_up, "dp", [(d, (d + 1) % ways) for d in range(ways)])
+        gathered = lax.dynamic_update_slice_in_dim(
+            gathered, going_up, (here - far) % ways * step, axis=0
+        )
+        if 2 * far < ways:
+            going_down = lax.ppermute(going_down, "dp", [(d, (d - 1) % ways) for d in range(ways)])
+            gathered = lax.dynamic_update_slice_in_dim(
+                gathered, going_down, (here + far) % ways * step, axis=0
+            )
     grad_pre = gathered[:, :hidden]
     grad_lin = gathered[:, hidden : 2 * hidden]
     activated = gathered[:, 2 * hidden :]

time: 349 us -> 354 us (1.014)
  waiting for transfers between devices: 150 us -> 141 us
  local copies, waits for them, and re-layouts: 25.7 us -> 32.8 us
    all_gather x1 -> x0, waiting for transfers between devices: 45.8 us -> none  [shards(): lax.all_gather(jnp.concatenate([grad_pre, grad_lin, activated], axis=1),...]
    ppermute x0 -> x3, waiting for transfers between devices: none -> 40.4 us  [the longest x2 40.4 us: shards(): lax.ppermute(going_up, 'dp', [(d, (d + 1) % ways) for d in range(ways)])]
    dynamic_update_slice x0 -> x3, local copies, waits for them, and re-layouts: none -> 4.69 us  [the longest x1 2.61 us: shards(): lax.dynamic_update_slice_in_dim(gathered, going_down, (here + far) % ways...]
  transfers between devices with their start and end apart: 3 -> 5, of which waited for: 3 -> 4; matrix products, arithmetic and copies ran while one was open for 5% -> 6% of each run, Pallas kernels for 0% -> 0%
where the time goes in v1:
time: 354 us; the launch traced here: 353 us
  waiting for transfers between devices  141 us (40%)
  blocking collectives  98.5 us (28%)
  matrix products  43 us (12%)
  local copies, waits for them, and re-layouts  32.8 us (9%)
  between operations  14.2 us (4%)
  starting transfers between devices  12 us (3%)
  other arithmetic  11 us (3%)
    all_to_all x1, blocking collectives, shards(): lax.all_to_all(flat_both, ('expert', 'dp'), split_axis=0, concat_axis=0,...  98.5 us
    reduce_scatter x1, waiting for transfers between devices, shards(): lax.psum_scatter(jnp.concatenate([gate_part, up_part, back_part], axis=1)...  72.4 us
    ppermute x2, waiting for transfers between devices, shards(): lax.ppermute(going_up, 'dp', [(d, (d + 1) % ways) for d in range(ways)])  40.4 us
    all_to_all x1, waiting for transfers between devices, shards(): lax.all_to_all(flat_back, ('expert', 'dp'), split_axis=0, concat_axis=0,...  28.4 us
    dot_general x5, matrix products, contract_rows(): lax.dot_general(left, right, (((0,), (0,)), ((), ())), preferred_element_...  23.4 us
    all_to_all x1, starting transfers between devices, shards(): lax.all_to_all(flat_back, ('expert', 'dp'), split_axis=0, concat_axis=0,...  9.33 us
    reshape x1, local copies, waits for them, and re-layouts, shards(): recv_both = recv_both.reshape(buffer_rows, 2 * slice_width)  8.11 us
  transfers between devices with their start and end apart: 5, of which 4 were waited for; matrix products, arithmetic and copies ran while one was open for 6% of the time, Pallas kernels for 0%

profile of v1, /device:TPU:1, one launch (start us, length us, event | category | flops | bytes accessed | tf_op | source)
XLA Modules:
  0.0 352.8 jit_solution(16507439965754084810)
XLA Ops:
  7.2 0.0 copy-start
  7.2 0.0 reduce-scatter.2.cloned.1.call-start
  7.2 0.8 copy.28
  8.0 0.1 eq.32
  8.1 0.1 fusion.29
  8.2 0.0 copy-start.3
  8.2 0.2 reduce_window_sum.11
  8.4 0.2 select_reduce_fusion.1
  8.6 0.1 reduce_sum.21
  8.7 0.1 fusion.28
  8.8 0.8 copy.30
  9.6 0.1 select_reduce_fusion
  9.7 0.0 copy-done
  9.7 2.2 fusion
  11.9 3.5 reshape.40
  15.4 0.0 copy-done.3
  15.4 2.2 convolution_convert_fusion
  17.6 4.6 %reshape.39 = bf16[32,5,4,1792]{3,2,1,0:T(4,128)(2,1)} reshape(bf16[160,7168]{1,0:T(8,128)(2,1)} %convolution_convert_fusion) | data formatting | bytes 4587520 | tf_op jit(solution)/shard_map/reshape | solution.py:45
  22.2 3.7 %maximum_bitcast_fusion = bf16[32,4,5,3584]{3,1,2,0:T(4,128)(2,1)S(1)} fusion(bf16[32,5,4,1792]{3,2,1,0:T(4,128)(2,1)S(1)} %reshape.40, bf16[32,5,4,1792]{3,2,1,0:T(4,128)(2,1)} %reshape.39), kind=kLoop, calls=%fused_computation.5 | loop fusion | flops 9175040 | bytes 9175040 | tf_op jit(solution)/shard_map/transpose | solution.py:48
  25.9 1.7 copy.36
  27.6 98.5 %all_to_all.10 = bf16[128,5,3584]{2,1,0:T(8,128)(2,1)} all-to-all(bf16[128,5,3584]{2,1,0:T(8,128)(2,1)S(1)} %bitcast.36), channel_id=1, replica_groups=mesh['expert'=32,'dp'=4] {'expert','dp'}, dimensions={0} | all-to-all | bytes 9175040 | tf_op jit(solution)/shard_map/all_to_all | solution.py:49
  126.1 8.1 %reshape.42 = bf16[640,3584]{1,0:T(8,128)(2,1)} reshape(bf16[128,5,3584]{2,1,0:T(8,128)(2,1)} %all_to_all.10) | data formatting | bytes 9175040 | tf_op jit(solution)/shard_map/reshape | solution.py:50
  134.2 0.0 copy-start.2
  134.2 0.0 copy-start.4
  134.2 5.4 %fusion.1 = f32[640,1024]{1,0:T(8,128)S(1)} fusion(bf16[1,1024,1792]{2,1,0:T(8,128)(2,1)} %param.13, bf16[640,3584]{1,0:T(8,128)(2,1)} %reshape.42), kind=kOutput, calls=%fused_computation.10 | convolution fusion | flops 2348810240 | bytes 8585216 | tf_op jit(solution)/shard_map/dot_general | solution.py:58
  139.7 0.0 copy-done.2
  139.7 0.0 copy-done.4
  139.7 0.0 copy-start.6
  139.7 2.5 fusion.5
  142.2 0.0 copy-done.6
  142.2 2.5 fusion.9
  144.8 3.4 pad_maximum_fusion
  148.2 0.0 reduce-scatter.2.cloned.1.call-update
  148.2 72.4 %reduce-scatter.2.cloned.1.call-done = f32[160,3072]{1,0:T(8,128)} async-done(((f32[640,3072]{1,0:T(8,128)}), f32[160,3072]{1,0:T(8,128)}) %reduce-scatter.2.cloned.1.call-update) | async-done | bytes 1966096 | tf_op jit(solution)/shard_map/reduce_scatter | solution.py:61
  220.7 1.9 multiply_convert_fusion.2
  222.6 2.4 broadcast_in_dim.28
  225.0 1.2 pad_maximum_fusion.1
  226.2 0.0 collective-permute-start
  226.2 2.7 collective-permute-start.1
  228.9 21.1 %collective-permute-done = bf16[160,3072]{1,0:T(8,128)(2,1)S(1)} collective-permute-done((bf16[160,3072]{1,0:T(8,128)(2,1)S(1)}, bf16[160,3072]{1,0:T(8,128)(2,1)S(1)}, u32[]{:S(2)}, u32[]{:S(2)}) %collective-permute-start) | collective-permute-done | bytes 983072 | tf_op jit(solution)/shard_map/ppermute | solution.py:78
  250.0 0.0 collective-permute-start.2
  250.0 0.0 copy-start.5
  250.0 1.1 constant_dynamic-update-slice_fusion.1
  251.1 0.0 collective-permute-done.1
  251.1 2.6 constant_dynamic-update-slice_fusion
  253.7 19.3 %collective-permute-done.2 = bf16[160,3072]{1,0:T(8,128)(2,1)S(1)} collective-permute-done((bf16[160,3072]{1,0:T(8,128)(2,1)S(1)}, bf16[160,3072]{1,0:T(8,128)(2,1)S(1)}, u32[]{:S(2)}, u32[]{:S(2)}) %collective-permute-start.2) | collective-permute-done | bytes 983072 | tf_op jit(solution)/shard_map/ppermute | solution.py:78
  272.9 1.0 constant_dynamic-update-slice_fusion.3
  273.9 0.0 copy-done.5
  273.9 4.0 %fusion.3 = f32[640,1792]{1,0:T(8,128)S(1)} fusion(bf16[1,1792,1024]{2,1,0:T(8,128)(2,1)S(1)} %copy-done.5, bf16[640,3072]{1,0:T(8,128)(2,1)} %constant_dynamic-update-slice_fusion.3), kind=kOutput, calls=%fused_computation.12 | convolution fusion | flops 2348810240 | bytes 9568256 | tf_op jit(solution)/shard_map/dot_general | solution.py:92
  278.0 0.0 copy-done.7
  278.0 3.9 %add_convert_fusion = bf16[640,1792]{1,0:T(8,128)(2,1)S(1)} fusion(f32[640,1792]{1,0:T(8,128)S(1)} %fusion.3, bf16[1,1792,1024]{2,1,0:T(8,128)(2,1)S(1)} %copy-done.7, bf16[640,3072]{1,0:T(8,128)(2,1)} %constant_dynamic-update-slice_fusion.3), kind=kOutput, calls=%fused_computation.6 | convolution fusion | flops 2351104000 | bytes 11862016 | tf_op jit(solution)/shard_map/dot_general | solution.py:90
  281.9 2.7 reshape.43
  284.6 9.3 %all-to-all-start.1 = ((bf16[128,5,1792]{2,1,0:T(8,128)(2,1)}), bf16[128,5,1792]{2,1,0:T(8,128)(2,1)}, u32[]{:S(2)}, u32[]{:S(2)}) async-start(bf16[128,5,1792]{2,1,0:T(8,128)(2,1)} %reshape.43), calls=%async_computation.2 | async-start | bytes 7340032 | tf_op jit(solution)/shard_map/all_to_all | solution.py:100
  294.0 0.0 slice-start.1
  294.0 7.1 %fusion.11 = bf16[1,1792,1024]{2,1,0:T(8,128)(2,1)} fusion(bf16[640,3584]{1,0:T(8,128)(2,1)} %reshape.42, bf16[640,3072]{1,0:T(8,128)(2,1)} %constant_dynamic-update-slice_fusion.3), kind=kOutput, calls=%fused_computation.20 | convolution fusion | flops 2350645248 | bytes 7274496 | tf_op jit(solution)/shard_map/dot_general | solution.py:17
  301.0 0.0 slice-done
  301.0 0.0 slice-done.1
  301.0 5.8 %fusion.12 = bf16[1,1792,1024]{2,1,0:T(8,128)(2,1)} fusion(bf16[640,3584]{1,0:T(8,128)(2,1)S(1)} %bitcast.40, bf16[640,3072]{1,0:T(8,128)(2,1)} %constant_dynamic-update-slice_fusion.3), kind=kOutput, calls=%fused_computation.21 | convolution fusion | flops 2350645248 | bytes 7274496 | tf_op jit(solution)/shard_map/dot_general | solution.py:17
  306.9 6.2 %fusion.13 = bf16[1,1024,1792]{2,1,0:T(8,128)(2,1)} fusion(bf16[640,3584]{1,0:T(8,128)(2,1)S(1)} %bitcast.40, bf16[640,3072]{1,0:T(8,128)(2,1)} %constant_dynamic-update-slice_fusion.3), kind=kOutput, calls=%fused_computation.22 | convolution fusion | flops 2350645248 | bytes 7274496 | tf_op jit(solution)/shard_map/dot_general | solution.py:17
  313.0 28.4 %all-to-all-done.1 = bf16[128,5,1792]{2,1,0:T(8,128)(2,1)} async-done(((bf16[128,5,1792]{2,1,0:T(8,128)(2,1)}), bf16[128,5,1792]{2,1,0:T(8,128)(2,1)}, u32[]{:S(2)}, u32[]{:S(2)}) %all-to-all-start.1) | async-done | bytes 2293792 | tf_op jit(solution)/shard_map/all_to_all | solution.py:100
  341.5 3.0 copy.34
  344.5 0.3 copy.38
  344.8 1.1 convolution_convert_fusion.1
  345.9 0.0 copy-done.1
  (5 shorter events, 0.0 us)
Async XLA Ops:
  7.2 2.5 copy-start
  7.2 213.5 %reduce-scatter.2.cloned.1.call-start = ((), (), s32[]{:S(2)}) async-start(), calls=%async_computation.3 | async-start | bytes 9830400 | tf_op jit(solution)/shard_map/reduce_scatter | solution.py:61
  8.2 7.2 %copy-start.3 = (bf16[16,7168]{1,0:T(8,128)(2,1)S(1)}, bf16[16,7168]{1,0:T(8,128)(2,1)}, u32[]{:S(2)}) copy-start(bf16[16,7168]{1,0:T(8,128)(2,1)} %param.7) | copy-start | bytes 688132
  134.2 5.4 %copy-start.2 = (bf16[640,3584]{1,0:T(8,128)(2,1)S(1)}, bf16[640,3584]{1,0:T(8,128)(2,1)}, u32[]{:S(2)}) copy-start(bf16[640,3584]{1,0:T(8,128)(2,1)} %reshape.42) | copy-start | bytes 13762564
  134.2 5.5 %copy-start.4 = (bf16[1,1792,1024]{2,1,0:T(8,128)(2,1)S(1)}, bf16[1,1792,1024]{2,1,0:T(8,128)(2,1)}, u32[]{:S(2)}) copy-start(bf16[1,1792,1024]{2,1,0:T(8,128)(2,1)} %param.12) | copy-start | bytes 11010052
  139.7 2.5 copy-start.6
  226.2 23.8 %collective-permute-start = (bf16[160,3072]{1,0:T(8,128)(2,1)S(1)}, bf16[160,3072]{1,0:T(8,128)(2,1)S(1)}, u32[]{:S(2)}, u32[]{:S(2)}) collective-permute-start(bf16[160,3072]{1,0:T(8,128)(2,1)S(1)} %get-tuple-element.7), channel_id=1, source_target_pairs={{0,1},{1,2},{2,3},{3,0},{4,5},{5,6},{6,7},{7,4},{8,9},{9,10},{10,1... | collective-permute-start | bytes 2949128 | tf_op jit(solution)/shard_map/ppermute | solution.py:78
  226.2 24.9 %collective-permute-start.1 = (bf16[160,3072]{1,0:T(8,128)(2,1)S(1)}, bf16[160,3072]{1,0:T(8,128)(2,1)}, u32[]{:S(2)}, u32[]{:S(2)}) collective-permute-start(bf16[160,3072]{1,0:T(8,128)(2,1)S(1)} %get-tuple-element.7), channel_id=1, source_target_pairs={{0,3},{1,0},{2,1},{3,2},{4,7},{5,4},{6,5},{7,6},{8,11},{9,8},{10,9... | collective-permute-start | bytes 2949128 | tf_op jit(solution)/shard_map/ppermute | solution.py:83
  250.0 22.9 %collective-permute-start.2 = (bf16[160,3072]{1,0:T(8,128)(2,1)S(1)}, bf16[160,3072]{1,0:T(8,128)(2,1)S(1)}, u32[]{:S(2)}, u32[]{:S(2)}) collective-permute-start(bf16[160,3072]{1,0:T(8,128)(2,1)S(1)} %collective-permute-done), channel_id=1, source_target_pairs={{0,1},{1,2},{2,3},{3,0},{4,5},{5,6},{6,7},{7,4},{8,9},{9,10},{10,1... | collective-permute-start | bytes 2949128 | tf_op jit(solution)/shard_map/ppermute | solution.py:78
  250.0 23.9 %copy-start.5 = (bf16[1,1792,1024]{2,1,0:T(8,128)(2,1)S(1)}, bf16[1,1792,1024]{2,1,0:T(8,128)(2,1)}, u32[]{:S(2)}) copy-start(bf16[1,1792,1024]{2,1,0:T(8,128)(2,1)} %param.12) | copy-start | bytes 11010052
  273.9 4.0 %copy-start.7 = (bf16[1,1792,1024]{2,1,0:T(8,128)(2,1)S(1)}, bf16[1,1792,1024]{2,1,0:T(8,128)(2,1)}, u32[]{:S(2)}) copy-start(bf16[1,1792,1024]{2,1,0:T(8,128)(2,1)} %param.11) | copy-start | bytes 11010052
  284.6 16.4 %slice-start = ((s8[4587520]{0:T(1024)(128)(4,1)}), s8[393216]{0:T(1024)(128)(4,1)S(1)}, s32[]{:S(2)}) async-start(s8[4587520]{0:T(1024)(128)(4,1)} %bitcast.39), calls=%async_computation.4 | async-start | bytes 786432
  284.6 56.9 %all-to-all-start.1 = ((bf16[128,5,1792]{2,1,0:T(8,128)(2,1)}), bf16[128,5,1792]{2,1,0:T(8,128)(2,1)}, u32[]{:S(2)}, u32[]{:S(2)}) async-start(bf16[128,5,1792]{2,1,0:T(8,128)(2,1)} %reshape.43), calls=%async_computation.2 | async-start | bytes 7340032 | tf_op jit(solution)/shard_map/all_to_all | solution.py:100
  294.0 7.1 %slice-start.1 = ((s8[4587520]{0:T(1024)(128)(4,1)}), s8[4194304]{0:T(1024)(128)(4,1)S(1)}, s32[]{:S(2)}) async-start(s8[4587520]{0:T(1024)(128)(4,1)} %bitcast.39), calls=%async_computation.5 | async-start | bytes 8388608
  341.5 4.5 %copy-start.1 = (bf16[16,7168]{1,0:T(8,128)(2,1)S(1)}, bf16[16,7168]{1,0:T(8,128)(2,1)}, u32[]{:S(2)}) copy-start(bf16[16,7168]{1,0:T(8,128)(2,1)} %param.8) | copy-start | bytes 688132
Sparse Core Ops, SparseCore 0:
  148.3 72.2 reduce-scatter.1
